TPU v7x, 128 devices: a whole 4x4x4 slice. The times are simulated.
128 devices in a mesh: scan: 8 (over z, x_lo), det: 16 (over y, x_hi, core).
Axes of the slice: x: 4 (x_hi: 2, x_lo: 2; x = x_hi * 2 + x_lo), y: 4, z: 4, core: 2. Of those that a mesh axis runs over, the one named last changes fastest.
Arguments:
- frames: bfloat16 [16, 1024, 16384], P('det', 'scan'), may hold values from -6 to 6
- offsets: int32 [16384, 2], P(('scan', 'det')), may hold values from -32 to 32
- bright: int32 [16384], P(('scan', 'det')), may hold values from 0 to 1, as said below
- aberration: float32 [2], replicated, may hold values from 0.5 to 2
Outputs:
- tiles: float32 [16, 8, 160], P('det', 'scan')
Inputs may be any that keep to these rules, and one draw needn't show every extreme that they name: bright[k] is 1 exactly where (k // 128 - a)^2 + (k % 128 - b)^2 <= R^2 and 0 elsewhere, for one centre with whole a in 62 .. 66 and whole b in 62 .. 66, and one whole radius R in 40 .. 56, all ranges inclusive; so at least one pixel is 1.
All inputs are finite; a program needn't handle non-finite values.
Results may differ from a plain program's by a relative error of at most 0.0023.
Values may be sent and summed in bfloat16 or wider, within the bound.
No kernel may reach another device: no remote copies, remote signals or barrier semaphores. Data moves between devices by JAX's collectives and lax.ppermute only.
A program may use at most 128 MiB of HBM per device.

v0:
```python
import math

import jax
import jax.numpy as jnp
from jax import lax
from jax.sharding import PartitionSpec as P

SR = 16
SC = 1024
DROWS = 128
DCOLS = 128
HALO = 16


TWO_PI = 2.0 * math.pi
EXACT_PRECISION = lax.Precision.HIGHEST


def extended(cells, sides, width):
    for axis, dim in sides:
        count = lax.axis_size(axis)
        head = lax.slice_in_dim(cells, 0, width, axis=dim)
        tail = lax.slice_in_dim(cells, cells.shape[dim] - width, cells.shape[dim], axis=dim)
        cells = jnp.concatenate(
            [
                lax.ppermute(tail, axis, [(i, (i + 1) % count) for i in range(count)]),
                cells,
                lax.ppermute(head, axis, [((i + 1) % count, i) for i in range(count)]),
            ],
            axis=dim,
        )
    return cells


def phase_angles(first, second_operand, modulus):
    product = jnp.mod(first[:, None] * second_operand[None, :], modulus)
    return TWO_PI / modulus * product.astype(jnp.float32)


def signed_frequency(length):
    position = jnp.arange(length, dtype=jnp.int32)
    folded = jnp.where(position < length // 2, position, position - length)
    return 2.0 * folded.astype(jnp.float32) / length


def pixel_phase(pixel_index, shifts, aberration):
    freq_rows = signed_frequency(SR)[:, None, None]
    freq_cols = signed_frequency(SC)[None, :, None]
    half_rows = DROWS // 2
    half_cols = DCOLS // 2
    tilt_x = ((pixel_index // DCOLS - half_rows).astype(jnp.float32) / half_rows)[None, None, :]
    tilt_y = ((pixel_index % DCOLS - half_cols).astype(jnp.float32) / half_cols)[None, None, :]
    ramp_rows = jnp.mod(jnp.arange(SR, dtype=jnp.int32)[:, None] * shifts[:, 0][None, :], SR)
    ramp_cols = jnp.mod(jnp.arange(SC, dtype=jnp.int32)[:, None] * shifts[:, 1][None, :], SC)
    shift_phase = (
        TWO_PI / SR * ramp_rows.astype(jnp.float32)[:, None, :]
        + TWO_PI / SC * ramp_cols.astype(jnp.float32)[None, :, :]
    )
    tilt_sq = tilt_x * tilt_x + tilt_y * tilt_y
    tilt_dot = tilt_x * freq_rows + tilt_y * freq_cols
    moved_x = freq_rows + tilt_x
    moved_y = freq_cols + tilt_y
    moved_sq = moved_x * moved_x + moved_y * moved_y
    lens_phase = math.pi * (
        aberration[0] * (freq_rows * freq_rows + freq_cols * freq_cols)
        + aberration[1] * (moved_sq * moved_sq - tilt_sq * tilt_sq - 4.0 * tilt_sq * tilt_dot)
    )
    return shift_phase - lens_phase


def window_weights(width):
    position = jnp.arange(width, dtype=jnp.int32)
    nearest = jnp.minimum(position, width - 1 - position)
    ramped = 0.3 + 0.35 * (
        1.0 - jnp.cos(math.pi * (nearest.astype(jnp.float32) + 0.5) / (2 * HALO))
    )
    return jnp.where(nearest < 2 * HALO, ramped, jnp.float32(1.0))


def tile_pictures(spec_real, spec_imag, columns, rows):
    col_angles = phase_angles(jnp.arange(SC, dtype=jnp.int32), columns.reshape(-1), SC).reshape(
        SC, columns.shape[0], columns.shape[1]
    )
    cos_cols = jnp.cos(col_angles)
    sin_cols = jnp.sin(col_angles)
    real_piece = jnp.einsum(
        "sq,qaw->saw", spec_real, cos_cols, precision=EXACT_PRECISION
    ) - jnp.einsum("sq,qaw->saw", spec_imag, sin_cols, precision=EXACT_PRECISION)
    imaginary_piece = jnp.einsum(
        "sq,qaw->saw", spec_real, sin_cols, precision=EXACT_PRECISION
    ) + jnp.einsum("sq,qaw->saw", spec_imag, cos_cols, precision=EXACT_PRECISION)
    angles_by_row = phase_angles(jnp.arange(SR, dtype=jnp.int32), rows.reshape(-1), SR).reshape(
        SR, rows.shape[0], rows.shape[1]
    )
    row_cosines = jnp.cos(angles_by_row)
    row_sines = jnp.sin(angles_by_row)
    return jnp.einsum(
        "mzq,mhl->hzql", row_cosines, real_piece, precision=EXACT_PRECISION
    ) - jnp.einsum("mzq,mhl->hzql", row_sines, imaginary_piece, precision=EXACT_PRECISION)


def local(frames, offsets, bright, aberration):
    scan_size = lax.axis_size("scan")
    det_size = lax.axis_size("det")
    rows_dev, tile, detector = frames.shape
    owned = offsets.shape[0]
    owner = lax.axis_index("scan") * det_size + lax.axis_index("det")
    bright_sum = lax.psum(jnp.sum(bright.astype(jnp.float32)), ("scan", "det"))
    layered = frames.reshape(1, rows_dev, tile, detector)
    arrived = lax.all_to_all(layered, ("scan", "det"), split_axis=3, concat_axis=0, tiled=True)
    images = arrived.reshape(scan_size, det_size, rows_dev, tile, owned)
    full_cols = jnp.arange(SC, dtype=jnp.int32)
    col_angles = phase_angles(full_cols, full_cols, SC)
    col_cos = jnp.cos(col_angles).astype(jnp.bfloat16).reshape(scan_size, tile, SC)
    col_sin = jnp.sin(col_angles).astype(jnp.bfloat16).reshape(scan_size, tile, SC)
    real_col = jnp.einsum(
        "abrcp,acq->brqp", images, col_cos, preferred_element_type=jnp.float32
    ).reshape(SR, SC, owned)
    imag_col = -jnp.einsum(
        "abrcp,acq->brqp", images, col_sin, preferred_element_type=jnp.float32
    ).reshape(SR, SC, owned)
    full_rows = jnp.arange(SR, dtype=jnp.int32)
    angles_by_row = phase_angles(full_rows, full_rows, SR)
    row_cos = jnp.cos(angles_by_row)
    row_sin = jnp.sin(angles_by_row)
    real_full = jnp.einsum(
        "rs,rqp->sqp", row_cos, real_col, precision=EXACT_PRECISION
    ) + jnp.einsum("rs,rqp->sqp", row_sin, imag_col, precision=EXACT_PRECISION)
    imag_full = jnp.einsum(
        "rs,rqp->sqp", row_cos, imag_col, precision=EXACT_PRECISION
    ) - jnp.einsum("rs,rqp->sqp", row_sin, real_col, precision=EXACT_PRECISION)
    pixel_index = owner * owned + jnp.arange(owned, dtype=jnp.int32)
    phase = pixel_phase(pixel_index, offsets, aberration)
    weights = bright.astype(jnp.float32)
    turn_cos = jnp.cos(phase) * weights
    turn_sin = jnp.sin(phase) * weights
    spec_real = jnp.sum(real_full * turn_cos - imag_full * turn_sin, axis=2)
    spec_imag = jnp.sum(real_full * turn_sin + imag_full * turn_cos, axis=2)
    width = tile + 2 * HALO
    tile_index = jnp.arange(scan_size, dtype=jnp.int32)
    row_groups = (
        jnp.arange(det_size, dtype=jnp.int32)[:, None] * rows_dev
        + jnp.arange(rows_dev, dtype=jnp.int32)[None, :]
    )
    plain_cols = tile_index[:, None] * tile + jnp.arange(tile, dtype=jnp.int32)[None, :]
    shares = tile_pictures(spec_real, spec_imag, plain_cols, row_groups).reshape(
        scan_size * det_size, rows_dev, tile
    )
    summed = lax.psum_scatter(shares, ("scan", "det"), scatter_dimension=0, tiled=True)
    bordered_tiles = extended(summed, (("scan", 2),), HALO)
    return (
        bordered_tiles
        * (1.0 / (SR * SC))
        / jnp.sqrt(bright_sum)
        * window_weights(width)[None, None, :]
    )


def solution(mesh):
    placed = (P("det", "scan", None), P(("scan", "det"), None), P(("scan", "det")), P())
    return jax.shard_map(
        local, mesh=mesh, in_specs=placed, out_specs=P("det", "scan", None), check_vma=False
    )
```

profile of v0, /device:TPU:0, one launch (start us, length us, event | category | flops | bytes accessed | tf_op | source)
XLA Modules:
  0.0 566.9 jit_solution(18203489787983127004)
XLA Ops:
  6.5 17.7 %copy.52 = bf16[1,1,128,16384]{2,1,0,3:T(2,128)(2,1)} copy(bf16[1,1,128,16384]{3,2,1,0:T(8,128)(2,1)} %bitcast.94) | data formatting | bytes 8388608 | tf_op jit(solution)/shard_map/reshape | solution.py:109
  24.8 90.7 %reduce = bf16[16384,128]{1,0:T(8,128)(2,1)} reduce(bf16[16384,1,1,128]{3,2,1,0:T(2,128)(2,1)} %bitcast.92, bf16[]{:T(256)} %broadcast.940), dimensions={1,2}, to_apply=%bitcast.82.reduce_sub_computation | reduce | bytes 8388610
  115.5 6.9 %reshape.577 = bf16[128,2,8192]{2,1,0:T(2,128)(2,1)} reshape(bf16[16384,128]{1,0:T(8,128)(2,1)} %reduce) | data formatting | bytes 8388608
  122.4 11.7 %all-to-all-start = ((bf16[128,2,8192]{2,1,0:T(2,128)(2,1)}), bf16[128,2,8192]{2,1,0:T(2,128)(2,1)}, u32[]{:S(2)}, u32[]{:S(2)}) async-start(bf16[128,2,8192]{2,1,0:T(2,128)(2,1)} %reshape.577), calls=%async_computation | async-start | bytes 8388608 | tf_op jit(solution)/shard_map/all_to_all | solution.py:110
  136.3 1.0 add_multiply_fusion
  137.3 48.4 %all-to-all-done = bf16[128,2,8192]{2,1,0:T(2,128)(2,1)} async-done(((bf16[128,2,8192]{2,1,0:T(2,128)(2,1)}), bf16[128,2,8192]{2,1,0:T(2,128)(2,1)}, u32[]{:S(2)}, u32[]{:S(2)}) %all-to-all-start) | async-done | bytes 4194336 | tf_op jit(solution)/shard_map/all_to_all | solution.py:110
  185.8 19.8 %reshape.578 = bf16[16384,1,1,128]{3,2,1,0:T(2,128)(2,1)} reshape(bf16[128,2,8192]{2,1,0:T(2,128)(2,1)} %all-to-all-done) | data formatting | bytes 8388608
  205.6 5.0 copy.78
  210.6 18.9 %convolution_bitcast_fusion = f32[16,1024,128]{2,1,0:T(8,128)S(1)} fusion(bf16[8,16,128,128]{2,3,1,0:T(8,128)(2,1)S(1)} %bitcast.95, s32[8,128]{1,0:T(8,128)S(1)} %multiply_add_fusion), kind=kOutput, calls=%fused_computation.35 | convolution fusion | flops 4310695936 | bytes 12587008 | tf_op jit(solution)/shard_map/abrcp,acq->brqp/dot_general | solution.py:116
  229.5 11.8 %fusion.5 = f32[16,1024,128]{2,0,1:T(8,128)S(1)} fusion(f32[16,1024,128]{2,1,0:T(8,128)S(1)} %convolution_bitcast_fusion), kind=kOutput, calls=%fused_computation.11 | convolution fusion | flops 402656768 | bytes 16777216 | tf_op jit(solution)/shard_map/rs,rqp->sqp/dot_general | solution.py:131
  241.3 12.0 %fusion.7 = f32[16,1024,128]{2,0,1:T(8,128)S(1)} fusion(f32[16,1024,128]{2,1,0:T(8,128)S(1)} %convolution_bitcast_fusion), kind=kOutput, calls=%fused_computation.13 | convolution fusion | flops 402656768 | bytes 16777216 | tf_op jit(solution)/shard_map/rs,rqp->sqp/dot_general | solution.py:126
  253.3 19.0 %fusion = f32[16,1024,128]{2,1,0:T(8,128)S(1)} fusion(bf16[8,16,128,128]{2,3,1,0:T(8,128)(2,1)S(1)} %bitcast.96, s32[8,128]{1,0:T(8,128)S(1)} %multiply_add_fusion), kind=kOutput, calls=%fused_computation.1 | convolution fusion | flops 4312793088 | bytes 12587008 | tf_op jit(solution)/shard_map/abrcp,acq->brqp/dot_general | solution.py:119
  272.3 11.8 %fusion.3 = f32[16,1024,128]{2,0,1:T(8,128)S(1)} fusion(f32[16,1024,128]{2,1,0:T(8,128)S(1)} %fusion), kind=kOutput, calls=%fused_computation.9 | convolution fusion | flops 402656768 | bytes 16777216 | tf_op jit(solution)/shard_map/rs,rqp->sqp/dot_general | solution.py:128
  284.1 53.7 %add_reduce_fusion = (f32[16,1024]{0,1:T(8,128)S(1)}, f32[16,1024]{0,1:T(8,128)S(1)}) fusion(f32[128]{0:T(128)S(1)} %convert_element_type.190, f32[1024,128]{1,0:T(8,128)} %get-tuple-element.8, f32[16,128]{1,0:T(8,128)S(1)} %get-tuple-element.12, f32[128]{0:T(128)S(1)} %get-tuple-element.19, f32[128]{0:T(128)S(1)} %get-tuple-element.20, ...), kind=kOutput, calls=%fused_computation.2 | convolution fusion | flops 450858496 | bytes 35350020 | tf_op jit(solution)/shard_map/rs,rqp->sqp/dot_general | solution.py:129
  337.8 18.4 %fusion.29 = f32[16,8,128]{2,0,1:T(8,128)S(1)} fusion(s32[8,128]{1,0:T(8,128)S(1)} %iota_add_fusion, f32[16,1024]{0,1:T(8,128)S(1)} %get-tuple-element.6), kind=kOutput, calls=%fused_computation.41 | convolution fusion | flops 216006656 | bytes 135168 | tf_op jit(solution)/shard_map/sq,qaw->saw/dot_general | solution.py:86
  356.2 18.6 %fusion.27 = f32[16,8,128]{2,0,1:T(8,128)S(1)} fusion(s32[8,128]{1,0:T(8,128)S(1)} %iota_add_fusion, f32[16,1024]{0,1:T(8,128)S(1)} %get-tuple-element.5), kind=kOutput, calls=%fused_computation.40 | convolution fusion | flops 216006656 | bytes 135168 | tf_op jit(solution)/shard_map/sq,qaw->saw/dot_general | solution.py:91
  374.8 18.5 %fusion.37 = f32[16,8,128]{2,0,1:T(8,128)S(1)} fusion(f32[16,8,128]{2,0,1:T(8,128)S(1)} %fusion.29, s32[8,128]{1,0:T(8,128)S(1)} %iota_add_fusion, f32[16,1024]{0,1:T(8,128)S(1)} %get-tuple-element.5), kind=kOutput, calls=%fused_computation.45 | convolution fusion | flops 216023040 | bytes 200704 | tf_op jit(solution)/shard_map/sq,qaw->saw/dot_general | solution.py:88
  393.5 18.7 %fusion.40 = f32[16,8,128]{2,0,1:T(8,128)S(1)} fusion(f32[16,8,128]{2,0,1:T(8,128)S(1)} %fusion.27, s32[8,128]{1,0:T(8,128)S(1)} %iota_add_fusion, f32[16,1024]{0,1:T(8,128)S(1)} %get-tuple-element.6), kind=kOutput, calls=%fused_computation.46 | convolution fusion | flops 216023040 | bytes 200704 | tf_op jit(solution)/shard_map/sq,qaw->saw/dot_general | solution.py:89
  412.3 0.9 convolution_subtract_fusion
  413.8 64.4 %psum.7 = f32[]{:T(128)} all-reduce(f32[]{:T(128)} %convert_reduce_fusion), channel_id=1, replica_groups=mesh['scan'=8,'det'=16] {'scan','det'}, use_global_device_ids=true, to_apply=%region_4.5 | all-reduce | flops 1 | bytes 8 | tf_op jit(solution)/shard_map/psum | solution.py:108
  478.8 70.1 %all-reduce.3.cloned.1.call-done = f32[128,1,128]{2,1,0:T(1,128)} async-done(((f32[128,1,128]{2,1,0:T(1,128)}), f32[128,1,128]{2,1,0:T(1,128)}) %all-reduce.3.cloned.1.call-update) | async-done | bytes 65552
  549.6 3.8 collective-permute-start.1
  553.5 1.3 collective-permute-done.1
  554.8 4.4 collective-permute-done
  (32 shorter events, 4.7 us)
Async XLA Ops:
  122.4 11.8 %copy-start.2 = (s32[128]{0:T(128)S(1)}, s32[128]{0:T(128)}, u32[]{:S(2)}) copy-start(s32[128]{0:T(128)} %param.6) | copy-start | bytes 1540
  122.4 11.8 %copy-start = (f32[2]{0:T(128)S(1)}, f32[2]{0:T(128)}, u32[]{:S(2)}) copy-start(f32[2]{0:T(128)} %param.7) | copy-start | bytes 28
  122.4 13.4 %copy-start.1 = (s32[128,2]{0,1:T(2,128)S(1)}, s32[128,2]{0,1:T(2,128)}, u32[]{:S(2)}) copy-start(s32[128,2]{0,1:T(2,128)} %param.5) | copy-start | bytes 3076
  122.4 63.4 %all-to-all-start = ((bf16[128,2,8192]{2,1,0:T(2,128)(2,1)}), bf16[128,2,8192]{2,1,0:T(2,128)(2,1)}, u32[]{:S(2)}, u32[]{:S(2)}) async-start(bf16[128,2,8192]{2,1,0:T(2,128)(2,1)} %reshape.577), calls=%async_computation | async-start | bytes 8388608 | tf_op jit(solution)/shard_map/all_to_all | solution.py:110
  134.1 414.9 %all-reduce.3.cloned.1.call-start = ((), (), s32[]{:S(2)}) async-start(), calls=%async_computation.1 | async-start | bytes 131072
  549.6 5.1 collective-permute-start.1
  553.5 5.7 %collective-permute-start = (f32[1,1,16]{2,1,0:T(1,128)S(1)}, f32[1,1,16]{2,1,0:T(1,128)S(1)}, u32[]{:S(2)}, u32[]{:S(2)}) collective-permute-start(f32[1,1,16]{2,1,0:T(1,128)S(1)} %get-tuple-element.13), channel_id=1, source_target_pairs={{0,16},{16,32},{32,48},{48,64},{64,80},{80,96},{96,112},{112,0},{1... | collective-permute-start | bytes 200 | tf_op jit(solution)/shard_map/ppermute | solution.py:26
Sparse Core Ops, SparseCore 0:
  413.3 135.6 all-reduce.2
where the time goes:
time: 574 us; the launch traced here: 567 us
  matrix products  202 us (35%)
  waiting for transfers between devices  124 us (22%)
  other arithmetic  94.2 us (16%)
  blocking collectives  64.4 us (11%)
  local copies, waits for them, and re-layouts  51.5 us (9%)
  starting transfers between devices  15.6 us (3%)
  between operations  14.5 us (3%)
    unnamed x1, other arithmetic  90.7 us
    unnamed x2, waiting for transfers between devices  70.1 us
    psum x1, blocking collectives, local(): bright_sum = lax.psum(jnp.sum(bright.astype(jnp.float32)), ('scan', 'det'))  64.4 us
    dot_general x1, matrix products, local(): jnp.einsum('rs,rqp->sqp', row_cos, imag_col, precision=EXACT_PRECISION)  53.7 us
    all_to_all x1, waiting for transfers between devices, local(): lax.all_to_all(layered, ('scan', 'det'), split_axis=3, concat_axis=0, til...  48.4 us
    unnamed x11, local copies, waits for them, and re-layouts  32.9 us
    dot_general x1, matrix products, local(): jnp.einsum('abrcp,acq->brqp', images, col_sin, preferred_element_type=jnp...  19 us
    dot_general x1, matrix products, local(): jnp.einsum('abrcp,acq->brqp', images, col_cos, preferred_element_type=jnp...  18.9 us
  transfers between devices with their start and end apart: 4, of which 4 were waited for; matrix products, arithmetic and copies ran while one was open for 1% of the time, Pallas kernels for 0%

commit v1 on v0

v1 whole, which is shorter than its diff:
```python
import math

import jax
import jax.numpy as jnp
from jax import lax
from jax.sharding import PartitionSpec as P

SR = 16
SC = 1024
DROWS = 128
DCOLS = 128
HALO = 16


TWO_PI = 2.0 * math.pi
EXACT_PRECISION = lax.Precision.HIGHEST


def phase_angles(first, second_operand, modulus):
    product = jnp.mod(first[:, None] * second_operand[None, :], modulus)
    return TWO_PI / modulus * product.astype(jnp.float32)


def signed_frequency(length):
    position = jnp.arange(length, dtype=jnp.int32)
    folded = jnp.where(position < length // 2, position, position - length)
    return 2.0 * folded.astype(jnp.float32) / length


def pixel_phase(pixel_index, shifts, aberration):
    freq_rows = signed_frequency(SR)[:, None, None]
    freq_cols = signed_frequency(SC)[None, :, None]
    half_rows = DROWS // 2
    half_cols = DCOLS // 2
    tilt_x = ((pixel_index // DCOLS - half_rows).astype(jnp.float32) / half_rows)[None, None, :]
    tilt_y = ((pixel_index % DCOLS - half_cols).astype(jnp.float32) / half_cols)[None, None, :]
    ramp_rows = jnp.mod(jnp.arange(SR, dtype=jnp.int32)[:, None] * shifts[:, 0][None, :], SR)
    ramp_cols = jnp.mod(jnp.arange(SC, dtype=jnp.int32)[:, None] * shifts[:, 1][None, :], SC)
    shift_phase = (
        TWO_PI / SR * ramp_rows.astype(jnp.float32)[:, None, :]
        + TWO_PI / SC * ramp_cols.astype(jnp.float32)[None, :, :]
    )
    tilt_sq = tilt_x * tilt_x + tilt_y * tilt_y
    tilt_dot = tilt_x * freq_rows + tilt_y * freq_cols
    moved_x = freq_rows + tilt_x
    moved_y = freq_cols + tilt_y
    moved_sq = moved_x * moved_x + moved_y * moved_y
    lens_phase = math.pi * (
        aberration[0] * (freq_rows * freq_rows + freq_cols * freq_cols)
        + aberration[1] * (moved_sq * moved_sq - tilt_sq * tilt_sq - 4.0 * tilt_sq * tilt_dot)
    )
    return shift_phase - lens_phase


def window_weights(width):
    position = jnp.arange(width, dtype=jnp.int32)
    nearest = jnp.minimum(position, width - 1 - position)
    ramped = 0.3 + 0.35 * (
        1.0 - jnp.cos(math.pi * (nearest.astype(jnp.float32) + 0.5) / (2 * HALO))
    )
    return jnp.where(nearest < 2 * HALO, ramped, jnp.float32(1.0))


def inverse_transform(spec_real, spec_imag, columns, rows):
    col_angles = phase_angles(jnp.arange(SC, dtype=jnp.int32), columns, SC)
    cos_cols = jnp.cos(col_angles)
    sin_cols = jnp.sin(col_angles)
    real_piece = jnp.dot(spec_real, cos_cols, precision=EXACT_PRECISION) - jnp.dot(
        spec_imag, sin_cols, precision=EXACT_PRECISION
    )
    imaginary_piece = jnp.dot(spec_real, sin_cols, precision=EXACT_PRECISION) + jnp.dot(
        spec_imag, cos_cols, precision=EXACT_PRECISION
    )
    angles_by_row = phase_angles(jnp.arange(SR, dtype=jnp.int32), rows, SR)
    row_cosines = jnp.cos(angles_by_row)
    row_sines = jnp.sin(angles_by_row)
    return jnp.dot(row_cosines.T, real_piece, precision=EXACT_PRECISION) - jnp.dot(
        row_sines.T, imaginary_piece, precision=EXACT_PRECISION
    )


def local(frames, offsets, bright, aberration):
    scan_size = lax.axis_size("scan")
    det_size = lax.axis_size("det")
    rows_dev, tile, detector = frames.shape
    owned = offsets.shape[0]
    groups = detector // owned
    owner = lax.axis_index("scan") * det_size + lax.axis_index("det")
    blocks = jnp.transpose(frames.reshape(rows_dev * tile, groups, owned), (1, 0, 2))
    arrived = lax.all_to_all(blocks, ("scan", "det"), split_axis=0, concat_axis=0, tiled=True)
    images = arrived.reshape(scan_size, det_size, rows_dev, tile, owned)
    full_cols = jnp.arange(SC, dtype=jnp.int32)
    col_angles = phase_angles(full_cols, full_cols, SC)
    col_cos = jnp.cos(col_angles).astype(jnp.bfloat16)
    col_sin = jnp.sin(col_angles).astype(jnp.bfloat16)
    table = jnp.concatenate([col_cos, -col_sin], axis=1).reshape(scan_size, tile, 2 * SC)
    both_col = jnp.einsum(
        "abrcp,acq->brqp", images, table, preferred_element_type=jnp.float32
    ).reshape(SR, 2 * SC, owned)
    real_col = both_col[:, :SC]
    imag_col = both_col[:, SC:]
    full_rows = jnp.arange(SR, dtype=jnp.int32)
    angles_by_row = phase_angles(full_rows, full_rows, SR)
    row_cos = jnp.cos(angles_by_row)
    row_sin = jnp.sin(angles_by_row)
    real_full = jnp.einsum(
        "rs,rqp->sqp", row_cos, real_col, precision=EXACT_PRECISION
    ) + jnp.einsum("rs,rqp->sqp", row_sin, imag_col, precision=EXACT_PRECISION)
    imag_full = jnp.einsum(
        "rs,rqp->sqp", row_cos, imag_col, precision=EXACT_PRECISION
    ) - jnp.einsum("rs,rqp->sqp", row_sin, real_col, precision=EXACT_PRECISION)
    pixel_index = owner * owned + jnp.arange(owned, dtype=jnp.int32)
    phase = pixel_phase(pixel_index, offsets, aberration)
    weights = bright.astype(jnp.float32)
    turn_cos = jnp.cos(phase) * weights
    turn_sin = jnp.sin(phase) * weights
    spec_real = jnp.sum(real_full * turn_cos - imag_full * turn_sin, axis=2)
    spec_imag = jnp.sum(real_full * turn_sin + imag_full * turn_cos, axis=2)
    packed = jnp.concatenate(
        [spec_real.reshape(-1), spec_imag.reshape(-1), jnp.sum(weights).reshape(1)]
    )
    total = lax.psum(packed, ("scan", "det"))
    spec_real = total[: SR * SC].reshape(SR, SC)
    spec_imag = total[SR * SC : 2 * SR * SC].reshape(SR, SC)
    bright_sum = total[2 * SR * SC]
    width = tile + 2 * HALO
    columns = jnp.mod(
        lax.axis_index("scan") * tile - HALO + jnp.arange(width, dtype=jnp.int32), SC
    )
    rows = lax.axis_index("det") * rows_dev + jnp.arange(rows_dev, dtype=jnp.int32)
    picture = inverse_transform(spec_real, spec_imag, columns, rows)
    return (
        (picture * (1.0 / (SR * SC)) / jnp.sqrt(bright_sum) * window_weights(width)[None, :])
        .reshape(rows_dev, 1, width)
    )


def solution(mesh):
    placed = (P("det", "scan", None), P(("scan", "det"), None), P(("scan", "det")), P())
    return jax.shard_map(
        local, mesh=mesh, in_specs=placed, out_specs=P("det", "scan", None), check_vma=False
    )
```

time: 574 us -> 373 us (0.65)
  matrix products: 202 us -> 130 us
  blocking collectives: 64.4 us -> 0 us
  other arithmetic: 94.2 us -> 37.3 us
  local copies, waits for them, and re-layouts: 51.5 us -> 16.7 us
  waiting for transfers between devices: 124 us -> 156 us
    psum x0 -> x1, waiting for transfers between devices: none -> 141 us  [local(): total = lax.psum(packed, ('scan', 'det'))]
    unnamed x1 -> x0, other arithmetic: 90.7 us -> none
    dot_general x8 -> x7, matrix products: 113 us -> 31.5 us  [the longest x1 13.4 us: local(): jnp.einsum('abrcp,acq->brqp', images, table, preferred_element_type=jnp.f...]
    unnamed x2 -> x1, waiting for transfers between devices: 70.1 us -> 0.02 us
    psum x1 -> x0, blocking collectives: 64.4 us -> none  [local(): bright_sum = lax.psum(jnp.sum(bright.astype(jnp.float32)), ('scan', 'det'))]
    all_to_all x1, waiting for transfers between devices: 48.4 us -> 15.3 us  [local(): lax.all_to_all(blocks, ('scan', 'det'), split_axis=0, concat_axis=0, tile...]
    unnamed x11 -> x15, local copies, waits for them, and re-layouts: 32.9 us -> 6.47 us
    reshape x1 -> x2, local copies, waits for them, and re-layouts: 17.7 us -> 0.04 us  [the longest x1 0.02 us: local(): spec_imag = total[SR * SC:2 * SR * SC].reshape(SR, SC)]
  transfers between devices with their start and end apart: 4 -> 2, of which waited for: 4 -> 2; matrix products, arithmetic and copies ran while one was open for 1% -> 10% of each run, Pallas kernels for 0% -> 0%
where the time goes in v1:
time: 373 us; the launch traced here: 366 us
  waiting for transfers between devices  156 us (42%)
  matrix products  130 us (35%)
  other arithmetic  37.3 us (10%)
  local copies, waits for them, and re-layouts  16.7 us (4%)
  between operations  14.5 us (4%)
  starting transfers between devices  11.7 us (3%)
    psum x1, waiting for transfers between devices, local(): total = lax.psum(packed, ('scan', 'det'))  141 us
    dot_general x1, matrix products, local(): jnp.einsum('rs,rqp->sqp', row_cos, imag_col, precision=EXACT_PRECISION)  54.1 us
    neg x1, other arithmetic, local(): -col_sin  16.9 us
    dot_general x1, matrix products, local(): jnp.einsum('rs,rqp->sqp', row_sin, imag_col, precision=EXACT_PRECISION)  16.7 us
    dot_general x1, matrix products, local(): jnp.einsum('rs,rqp->sqp', row_cos, real_col, precision=EXACT_PRECISION)  16.6 us
    convert_element_type x1, other arithmetic, local(): col_cos = jnp.cos(col_angles).astype(jnp.bfloat16)  15.5 us
    all_to_all x1, waiting for transfers between devices, local(): lax.all_to_all(blocks, ('scan', 'det'), split_axis=0, concat_axis=0, tile...  15.3 us
    dot_general x1, matrix products, local(): jnp.einsum('abrcp,acq->brqp', images, table, preferred_element_type=jnp.f...  13.4 us
  transfers between devices with their start and end apart: 2, of which 2 were waited for; matrix products, arithmetic and copies ran while one was open for 10% of the time, Pallas kernels for 0%

profile of v1, /device:TPU:0, one launch (start us, length us, event | category | flops | bytes accessed | tf_op | source)
XLA Modules:
  0.0 366.4 jit_solution(14988252802277870520)
XLA Ops:
  6.5 6.4 %copy.37 = bf16[1,128,16384]{1,2,0:T(8,128)(2,1)} copy(bf16[1,128,16384]{2,1,0:T(8,128)(2,1)} %param.4) | data formatting | bytes 8388608 | tf_op args[0]
  12.9 11.7 %all-to-all-start = ((bf16[128,128,128]{1,2,0:T(8,128)(2,1)}), bf16[128,128,128]{1,2,0:T(8,128)(2,1)}, u32[]{:S(2)}, u32[]{:S(2)}) async-start(bf16[128,128,128]{1,2,0:T(8,128)(2,1)} %bitcast.61), calls=%async_computation | async-start | bytes 8388608 | tf_op jit(solution)/shard_map/all_to_all | solution.py:90
  24.8 0.7 fusion.126
  25.4 0.7 add_multiply_fusion.1
  26.4 0.6 convert_reduce_fusion
  27.4 1.2 add_multiply_fusion
  28.6 15.5 %cosine_convert_fusion = bf16[8,128,1024]{1,2,0:T(8,128)(2,1)S(1)} fusion(s32[8,128]{1,0:T(8,128)S(1)} %multiply_add_fusion), kind=kLoop, calls=%fused_computation.25 | loop fusion | flops 15728640 | bytes 2101248 | tf_op jit(solution)/shard_map/convert_element_type | solution.py:94
  44.1 16.9 %fusion.18 = bf16[8,128,1024]{1,2,0:T(8,128)(2,1)} fusion(s32[8,128]{1,0:T(8,128)S(1)} %multiply_add_fusion), kind=kLoop, calls=%fused_computation.29 | loop fusion | flops 18874368 | bytes 2101248 | tf_op jit(solution)/shard_map/neg | solution.py:96
  61.0 15.3 %all-to-all-done = bf16[128,128,128]{1,2,0:T(8,128)(2,1)} async-done(((bf16[128,128,128]{1,2,0:T(8,128)(2,1)}), bf16[128,128,128]{1,2,0:T(8,128)(2,1)}, u32[]{:S(2)}, u32[]{:S(2)}) %all-to-all-start) | async-done | bytes 4194336 | tf_op jit(solution)/shard_map/all_to_all | solution.py:90
  76.3 13.4 %convolution_bitcast_fusion = f32[16,2048,128]{2,1,0:T(8,128)} fusion(bf16[8,16,128,128]{2,3,1,0:T(8,128)(2,1)} %bitcast.5, bf16[8,128,1024]{1,2,0:T(8,128)(2,1)} %fusion.18, bf16[8,128,1024]{1,2,0:T(8,128)(2,1)S(1)} %cosine_convert_fusion), kind=kOutput, calls=%fused_computation.13 | convolution fusion | flops 8598323200 | bytes 25165824 | tf_op jit(solution)/shard_map/abrcp,acq->brqp/dot_general | solution.py:97
  89.7 6.9 %fusion.124 = (f32[16,1024,128]{2,1,0:T(8,128)S(1)}, f32[16,1024,128]{2,1,0:T(8,128)S(1)}) fusion(f32[16,2048,128]{2,1,0:T(8,128)} %convolution_bitcast_fusion), kind=kLoop, calls=%fused_computation.169 | loop fusion | bytes 33554432 | tf_op jit(solution)/shard_map/slice | solution.py:100
  96.6 11.6 %fusion.4 = f32[16,1024,128]{2,0,1:T(8,128)S(1)} fusion(f32[16,1024,128]{2,1,0:T(8,128)S(1)} %get-tuple-element.7), kind=kOutput, calls=%fused_computation.9 | convolution fusion | flops 402656768 | bytes 16777216 | tf_op jit(solution)/shard_map/rs,rqp->sqp/dot_general | solution.py:111
  108.2 16.6 %fusion.6 = f32[16,1024,128]{2,0,1:T(8,128)} fusion(f32[16,1024,128]{2,1,0:T(8,128)S(1)} %get-tuple-element.7), kind=kOutput, calls=%fused_computation.11 | convolution fusion | flops 402656768 | bytes 16777216 | tf_op jit(solution)/shard_map/rs,rqp->sqp/dot_general | solution.py:106
  124.8 16.7 %fusion.2 = f32[16,1024,128]{2,0,1:T(8,128)} fusion(f32[16,1024,128]{2,1,0:T(8,128)S(1)} %get-tuple-element.8), kind=kOutput, calls=%fused_computation.7 | convolution fusion | flops 402656768 | bytes 16777216 | tf_op jit(solution)/shard_map/rs,rqp->sqp/dot_general | solution.py:108
  141.5 54.1 %subtract_reduce_fusion = (f32[16,1024]{0,1:T(8,128)S(1)}, f32[16,1024]{0,1:T(8,128)S(1)}) fusion(f32[128]{0:T(128)S(1)} %convert_element_type.122, f32[1024,128]{1,0:T(8,128)S(1)} %copy-done.2, f32[16,128]{1,0:T(8,128)S(1)} %get-tuple-element.16, f32[128]{0:T(128)S(1)} %get-tuple-element.21, f32[128]{0:T(128)S(1)} %get-tuple-element.22, ...), kind=kOutput, calls=%fused_computation.1 | convolution fusion | flops 450858496 | bytes 35350020 | tf_op jit(solution)/shard_map/rs,rqp->sqp/dot_general | solution.py:109
  196.0 1.3 pad_maximum_fusion
  197.3 140.5 %all-reduce.2.cloned.1.call-done = f32[32769]{0:T(1024)} async-done(((f32[32769]{0:T(1024)}), f32[32769]{0:T(1024)}) %all-reduce.2.cloned.1.call-update) | async-done | bytes 131092 | tf_op jit(solution)/shard_map/psum | solution.py:122
  337.8 0.9 fusion.125
  338.7 4.3 %fusion.31 = f32[16,160]{1,0:T(8,128)S(1)} fusion(f32[16,1024]{1,0:T(8,128)S(1)} %reshape.408, s32[160]{0:T(256)S(1)} %and_select_fusion), kind=kOutput, calls=%fused_computation.49 | convolution fusion | flops 33751040 | bytes 76416 | tf_op jit(solution)/shard_map/dot_general | solution.py:68
  343.1 4.4 %fusion.33 = f32[16,160]{1,0:T(8,128)S(1)} fusion(f32[16,1024]{1,0:T(8,128)S(1)} %reshape.408, s32[160]{0:T(256)S(1)} %and_select_fusion), kind=kOutput, calls=%fused_computation.50 | convolution fusion | flops 33751040 | bytes 76416 | tf_op jit(solution)/shard_map/dot_general | solution.py:71
  347.5 4.6 %convolution_subtract_fusion = f32[16,160]{1,0:T(8,128)S(1)} fusion(f32[16,160]{1,0:T(8,128)S(1)} %fusion.31, f32[16,1024]{1,0:T(8,128)S(1)} %reshape.409, s32[160]{0:T(256)S(1)} %and_select_fusion), kind=kOutput, calls=%fused_computation.34 | convolution fusion | flops 33753600 | bytes 86656 | tf_op jit(solution)/shard_map/dot_general | solution.py:68
  352.3 4.4 %convolution_add_fusion = f32[16,160]{1,0:T(8,128)S(1)} fusion(f32[16,160]{1,0:T(8,128)S(1)} %fusion.33, f32[16,1024]{1,0:T(8,128)S(1)} %reshape.409, s32[160]{0:T(256)S(1)} %and_select_fusion), kind=kOutput, calls=%fused_computation.33 | convolution fusion | flops 33753600 | bytes 86656 | tf_op jit(solution)/shard_map/dot_general | solution.py:71
  356.8 1.2 slice.40
  358.7 0.6 divide_multiply_fusion
  (36 shorter events, 1.5 us)
Async XLA Ops:
  6.5 18.2 %copy-start.5 = (s32[128]{0:T(128)S(1)}, s32[128]{0:T(128)}, u32[]{:S(2)}) copy-start(s32[128]{0:T(128)} %param.6) | copy-start | bytes 1540
  6.5 18.2 %copy-start.3 = (f32[2]{0:T(128)S(1)}, f32[2]{0:T(128)}, u32[]{:S(2)}) copy-start(f32[2]{0:T(128)} %param.7) | copy-start | bytes 28
  6.5 20.5 %copy-start.4 = (s32[128,2]{0,1:T(2,128)S(1)}, s32[128,2]{0,1:T(2,128)}, u32[]{:S(2)}) copy-start(s32[128,2]{0,1:T(2,128)} %param.5) | copy-start | bytes 3076
  12.9 63.3 %all-to-all-start = ((bf16[128,128,128]{1,2,0:T(8,128)(2,1)}), bf16[128,128,128]{1,2,0:T(8,128)(2,1)}, u32[]{:S(2)}, u32[]{:S(2)}) async-start(bf16[128,128,128]{1,2,0:T(8,128)(2,1)} %bitcast.61), calls=%async_computation | async-start | bytes 8388608 | tf_op jit(solution)/shard_map/all_to_all | solution.py:90
  24.7 313.2 %all-reduce.2.cloned.1.call-start = ((), (), s32[]{:S(2)}) async-start(), calls=%async_computation.1 | async-start | bytes 270336 | tf_op jit(solution)/shard_map/psum | solution.py:122
  124.8 16.7 %copy-start = (f32[16,1024,128]{2,0,1:T(8,128)S(1)}, f32[16,1024,128]{2,0,1:T(8,128)}, u32[]{:S(2)}) copy-start(f32[16,1024,128]{2,0,1:T(8,128)} %fusion.6) | copy-start | bytes 25165828
  124.8 16.7 %copy-start.1 = (f32[1024,128]{1,0:T(8,128)S(1)}, f32[1024,128]{1,0:T(8,128)}, u32[]{:S(2)}) copy-start(f32[1024,128]{1,0:T(8,128)} %get-tuple-element.11) | copy-start | bytes 1572868
  124.8 16.7 %copy-start.2 = (f32[1024,128]{1,0:T(8,128)S(1)}, f32[1024,128]{1,0:T(8,128)}, u32[]{:S(2)}) copy-start(f32[1024,128]{1,0:T(8,128)} %get-tuple-element.12) | copy-start | bytes 1572868
Sparse Core Ops, SparseCore 0:
  197.4 140.3 all-reduce.1
